TPU v7x, 128 devices: a whole 4x4x4 slice. The times are simulated.
128 devices in a mesh: grp: 8 (over z, core), dev: 16 (over y, x).
Axes of the slice: x: 4, y: 4, z: 4, core: 2. Of those that a mesh axis runs over, the one named last changes fastest.
Arguments:
- positions: float32 [3, 131072], P(None, ('grp', 'dev')), may hold values from -3 to 3
- velocities: float32 [3, 131072], P(None, ('grp', 'dev')), may hold values from -5 to 5
- accelerations: float32 [3, 131072], P(None, ('grp', 'dev')), may hold values from -3 to 3
- jerks: float32 [3, 131072], P(None, ('grp', 'dev')), may hold values from -3 to 3
- levels: int32 [131072], P(('grp', 'dev')), may hold values from 0 to 5
- counts: int32 [2, 128], replicated, may hold values from 1 to 256, 16384 in all within a row
- active_rows: int32 [2, 32768], P(None, ('grp', 'dev')), may hold values from 0 to 1023, as said below
Outputs:
- new_positions: float32 [3, 131072], P(None, ('grp', 'dev'))
- new_velocities: float32 [3, 131072], P(None, ('grp', 'dev'))
- new_accelerations: float32 [3, 131072], P(None, ('grp', 'dev'))
- new_jerks: float32 [3, 131072], P(None, ('grp', 'dev'))
Inputs may be any that keep to these rules, and one draw needn't show every extreme that they name: In each step the 128 counts sum to exactly 16384 and the largest of them is exactly 256. `active_rows`: for each step and device, the 256 entries of the device's slots are distinct indices of that device's own stars; only the first counts of them are live.
All inputs are finite; a program needn't handle non-finite values.
Results may differ from a plain program's by a relative error of at most 0.00022.
Values sent between devices are 32-bit elements; how exact they have to be, the bound alone decides.
No kernel may reach another device: no remote copies, remote signals or barrier semaphores. Data moves between devices by JAX's collectives and lax.ppermute only.
A program may use at most 128 MiB of HBM per device.

v0:
```python
import math
import jax
import jax.numpy as jnp
from jax import lax
from jax.sharding import PartitionSpec as P

tick_length = 1.0 / 128.0


def pair_block(targets, src_pos, src_vel, mass, soft_sq):
    gap_x = src_pos[0][None, :] - targets[0][:, None]
    gap_y = src_pos[1][None, :] - targets[1][:, None]
    gap_z = src_pos[2][None, :] - targets[2][:, None]
    drift_x = src_vel[0][None, :] - targets[3][:, None]
    drift_y = src_vel[1][None, :] - targets[4][:, None]
    drift_z = src_vel[2][None, :] - targets[5][:, None]
    squared = gap_x * gap_x + gap_y * gap_y + gap_z * gap_z + soft_sq
    inverse = lax.rsqrt(squared)
    weight = mass * inverse * inverse * inverse
    along = 3.0 * (gap_x * drift_x + gap_y * drift_y + gap_z * drift_z) * inverse * inverse
    return jnp.stack(
        [
            jnp.sum(weight * gap_x, axis=1),
            jnp.sum(weight * gap_y, axis=1),
            jnp.sum(weight * gap_z, axis=1),
            jnp.sum(weight * (drift_x - along * gap_x), axis=1),
            jnp.sum(weight * (drift_y - along * gap_y), axis=1),
            jnp.sum(weight * (drift_z - along * gap_z), axis=1),
        ]
    )


def block_terms(packed, src_pos, src_vel, mass, soft_sq):
    width, total = packed.shape
    block = math.gcd(total, 2048)
    grouped = packed.reshape(width, total // block, block).transpose(1, 0, 2)
    result = lax.map(lambda targets: pair_block(targets, src_pos, src_vel, mass, soft_sq), grouped)
    return result.transpose(1, 0, 2).reshape(width, total)


def predict(positions, velocities, accelerations, jerks, elapsed):
    span = elapsed[None, :]
    pred_pos = (
        positions
        + span * velocities
        + 0.5 * span * span * accelerations
        + span * span * span / 6.0 * jerks
    )
    pred_vel = velocities + span * accelerations + 0.5 * span * span * jerks
    return (pred_pos, pred_vel)


def correct(old_pos, old_vel, old_acc, old_jerk, force, jerk_new, span):
    span = span[None, :]
    new_vel = old_vel + 0.5 * span * (old_acc + force) + span * span / 12.0 * (old_jerk - jerk_new)
    new_pos = old_pos + 0.5 * span * (old_vel + new_vel) + span * span / 12.0 * (old_acc - force)
    return (new_pos, new_vel)


def shards(positions, velocities, accelerations, jerks, levels, counts, active_rows):
    devices_all = lax.axis_size("grp") * lax.axis_size("dev")
    my_rank = lax.axis_index("grp") * lax.axis_size("dev") + lax.axis_index("dev")
    star_dev = positions.shape[1]
    slot_cap = active_rows.shape[1]
    stars_all = star_dev * devices_all
    live_all = stars_all // 8
    mass = 1.0 / stars_all
    soft_sq = 0.0004 * (131072.0 / stars_all) ** (2.0 / 3.0)
    chunks = 4
    chunk = live_all // chunks
    last_time = -(jnp.left_shift(jnp.int32(1), levels) - 1).astype(jnp.float32) * tick_length
    for step in range(active_rows.shape[0]):
        now = (step + 1) * tick_length
        pred_pos, pred_vel = predict(positions, velocities, accelerations, jerks, now - last_time)
        rows = active_rows[step]
        targets = jnp.concatenate([pred_pos[:, rows], pred_vel[:, rows]], axis=0)
        step_counts = counts[step]
        own_count = step_counts[my_rank]
        inclusive = jnp.cumsum(step_counts).astype(jnp.int32)
        first = inclusive - step_counts
        place = jnp.arange(live_all, dtype=jnp.int32)
        owner = jnp.sum((inclusive[None, :] <= place[:, None]).astype(jnp.int32), axis=1)
        owner = jnp.minimum(owner, devices_all - 1)
        slot = owner * slot_cap + place - first[owner]
        gathered = lax.all_gather(targets[None], ("grp", "dev"), axis=0, tiled=True)
        flat = gathered.transpose(1, 0, 2).reshape(6, devices_all * slot_cap)
        compact = flat[:, slot]
        parts = []
        summed = None
        for c in range(chunks):
            piece = compact[:, c * chunk : (c + 1) * chunk]
            terms = block_terms(piece, pred_pos, pred_vel, mass, soft_sq)
            if summed is not None:
                terms, summed = lax.optimization_barrier((terms, summed))
                parts.append(summed)
            summed = lax.psum(terms, ("grp", "dev"))
        parts.append(summed)
        parts.append(jnp.zeros((6, slot_cap), jnp.float32))
        totals = jnp.concatenate(parts, axis=1)
        own = lax.dynamic_slice_in_dim(totals, first[my_rank], slot_cap, 1)
        span = now - last_time[rows]
        new_pos, new_vel = correct(
            positions[:, rows],
            velocities[:, rows],
            accelerations[:, rows],
            jerks[:, rows],
            own[:3],
            own[3:],
            span,
        )
        live = jnp.arange(slot_cap, dtype=jnp.int32) < own_count
        target = jnp.where(live, rows, star_dev)
        positions = positions.at[:, target].set(new_pos, mode="drop")
        velocities = velocities.at[:, target].set(new_vel, mode="drop")
        accelerations = accelerations.at[:, target].set(own[:3], mode="drop")
        jerks = jerks.at[:, target].set(own[3:], mode="drop")
        last_time = last_time.at[target].set(now, mode="drop")
    return (positions, velocities, accelerations, jerks)


def solution(mesh):
    placed = (
        P(None, ("grp", "dev")),
        P(None, ("grp", "dev")),
        P(None, ("grp", "dev")),
        P(None, ("grp", "dev")),
        P(("grp", "dev")),
        P(),
        P(None, ("grp", "dev")),
    )
    return jax.shard_map(
        shards,
        mesh=mesh,
        in_specs=placed,
        out_specs=(
            P(None, ("grp", "dev")),
            P(None, ("grp", "dev")),
            P(None, ("grp", "dev")),
            P(None, ("grp", "dev")),
        ),
        check_vma=False,
    )
```

profile of v0, /device:TPU:1, one launch (start us, length us, event | category | flops | bytes accessed | tf_op | source)
XLA Modules:
  0.0 1731.8 jit_solution(9103468403013295511)
XLA Ops:
  8.6 2.6 compare_select_fusion.4
  14.8 63.9 %all-gather.2 = f32[128,6,256]{2,1,0:T(8,128)S(1)} all-gather(f32[1,6,256]{2,1,0:T(8,128)S(1)} %maximum_bitcast_fusion), channel_id=2, replica_groups=mesh['grp'=8,'dev'=16] {'grp','dev'}, dimensions={0}, use_global_device_ids=true | all-gather | bytes 792576 | tf_op jit(solution)/shard_map/all_gather | solution.py:85
  78.7 8.4 copy.253
  87.8 2.3 convert_reduce_fusion.1
  90.3 97.2 %gather_fusion.6 = s32[16384]{0:T(1024)S(1)} fusion(s32[128]{0:T(128)S(1)} %get-tuple-element.734, s32[16384]{0:T(1024)S(1)} %broadcast_clamp_fusion.3), kind=kCustom, calls=%fused_computation.6 | custom fusion | bytes 196608 | tf_op jit(solution)/shard_map/gather | solution.py:84
  187.7 60.2 %gather_fusion.7 = f32[16384,6]{1,0:T(8,128)} fusion(f32[6,32768]{0,1:T(8,128)} %bitcast.632, s32[16384]{0:T(1024)S(1)} %broadcast_clamp_fusion.1), kind=kCustom, calls=%fused_computation.7 | custom fusion | bytes 851968 | tf_op jit(solution)/shard_map/gather | solution.py:87
  247.9 6.2 fusion.167
  254.0 2.2 copy.256
  256.3 32.8 %while.81 = (s32[]{:T(128)}, f32[2,6,2048]{2,1,0:T(8,128)S(1)}, f32[3,1024]{1,0:T(4,128)S(1)}, f32[2,6,2048]{2,1,0:T(8,128)S(1)}, f32[3,1024]{1,0:T(4,128)S(1)},...) while((s32[]{:T(128)}, f32[2,6,2048]{2,1,0:T(8,128)S(1)}, ...), condition=%wide.region_17.18_spmd, body=%wide.region_10.17_spmd.sunk | while | flops 85970952 | bytes 499925 | solution.py:37
  256.4 16.2 fusion.187
  272.8 16.2 fusion.187
  290.1 2.3 convert_reduce_fusion
  292.5 2.2 copy.255
  294.7 32.8 %while.80 = (s32[]{:T(128)}, f32[2,6,2048]{2,1,0:T(8,128)S(1)}, f32[3,1024]{1,0:T(4,128)S(1)}, f32[2,6,2048]{2,1,0:T(8,128)S(1)}, f32[3,1024]{1,0:T(4,128)S(1)},...) while((s32[]{:T(128)}, f32[2,6,2048]{2,1,0:T(8,128)S(1)}, ...), condition=%wide.region_9.10_spmd, body=%wide.region_2.9_spmd.sunk | while | flops 85970952 | bytes 499925 | solution.py:37
  294.8 16.2 fusion.185
  311.2 16.2 fusion.185
  327.5 2.3 copy.257
  329.8 32.8 %while.82 = (s32[]{:T(128)}, f32[2,6,2048]{2,1,0:T(8,128)S(1)}, f32[3,1024]{1,0:T(4,128)S(1)}, f32[2,6,2048]{2,1,0:T(8,128)S(1)}, f32[3,1024]{1,0:T(4,128)S(1)},...) while((s32[]{:T(128)}, f32[2,6,2048]{2,1,0:T(8,128)S(1)}, ...), condition=%wide.region_26.27_spmd, body=%wide.region_19.26_spmd.sunk | while | flops 85970952 | bytes 499925 | solution.py:37
  329.9 16.2 fusion.189
  346.4 16.2 fusion.189
  363.3 32.9 %while.83 = (s32[]{:T(128)}, f32[2,6,2048]{2,1,0:T(8,128)S(1)}, f32[3,1024]{1,0:T(4,128)S(1)}, f32[2,6,2048]{2,1,0:T(8,128)S(1)}, f32[3,1024]{1,0:T(4,128)S(1)},...) while((s32[]{:T(128)}, f32[2,6,2048]{2,1,0:T(8,128)S(1)}, ...), condition=%wide.region_35.36_spmd, body=%wide.region_28.35_spmd.sunk | while | flops 85970952 | bytes 499925 | solution.py:37
  363.4 16.2 fusion.191
  379.9 16.2 fusion.191
  396.2 1.4 gather_fusion.1
  397.6 1.9 scatter_fusion.1
  399.8 97.2 %gather_fusion.15 = s32[16384]{0:T(1024)S(1)} fusion(s32[128]{0:T(128)S(1)} %get-tuple-element.733, s32[16384]{0:T(1024)S(1)} %broadcast_clamp_fusion.2), kind=kCustom, calls=%fused_computation.15 | custom fusion | bytes 196608 | tf_op jit(solution)/shard_map/gather | solution.py:84
  497.1 1.4 gather_fusion.10
  509.3 137.8 %all-reduce.11.cloned.1.call-done = f32[6,4096]{1,0:T(8,128)} async-done(((f32[6,4096]{1,0:T(8,128)}), f32[6,4096]{1,0:T(8,128)}) %all-reduce.11.cloned.1.call-update) | async-done | bytes 98320 | tf_op jit(solution)/shard_map/psum | solution.py:96
  647.2 0.9 constant_dynamic-update-slice_fusion.3
  648.1 141.3 %all-reduce.13.cloned.1.call-done = f32[6,4096]{1,0:T(8,128)} async-done(((f32[6,4096]{1,0:T(8,128)}), f32[6,4096]{1,0:T(8,128)}) %all-reduce.13.cloned.1.call-update) | async-done | bytes 98320 | tf_op jit(solution)/shard_map/psum | solution.py:96
  789.5 0.9 constant_dynamic-update-slice_fusion.2
  790.4 141.8 %all-reduce.15.cloned.1.call-done = f32[6,4096]{1,0:T(8,128)} async-done(((f32[6,4096]{1,0:T(8,128)}), f32[6,4096]{1,0:T(8,128)}) %all-reduce.15.cloned.1.call-update) | async-done | bytes 98320 | tf_op jit(solution)/shard_map/psum | solution.py:96
  933.4 1.4 scatter_fusion
  934.9 1.4 scatter_fusion.3
  936.4 1.4 scatter_fusion.2
  937.9 1.4 scatter_fusion.4
  941.9 59.0 %all-gather.3 = f32[128,6,256]{2,1,0:T(8,128)S(1)} all-gather(f32[1,6,256]{2,1,0:T(8,128)S(1)} %maximum_bitcast_fusion.1), channel_id=3, replica_groups=mesh['grp'=8,'dev'=16] {'grp','dev'}, dimensions={0}, use_global_device_ids=true | all-gather | bytes 792576 | tf_op jit(solution)/shard_map/all_gather | solution.py:85
  1000.9 8.4 copy.274
  1009.3 60.2 %gather_fusion.16 = f32[16384,6]{1,0:T(8,128)} fusion(f32[6,32768]{0,1:T(8,128)} %bitcast.633, s32[16384]{0:T(1024)S(1)} %broadcast_clamp_fusion), kind=kCustom, calls=%fused_computation.16 | custom fusion | bytes 851968 | tf_op jit(solution)/shard_map/gather | solution.py:87
  1069.4 6.2 fusion.166
  1075.6 2.2 copy.276
  1077.9 32.8 %while.84 = (s32[]{:T(128)}, f32[2,6,2048]{2,1,0:T(8,128)S(1)}, f32[3,1024]{1,0:T(4,128)S(1)}, f32[2,6,2048]{2,1,0:T(8,128)S(1)}, f32[3,1024]{1,0:T(4,128)S(1)},...) while((s32[]{:T(128)}, f32[2,6,2048]{2,1,0:T(8,128)S(1)}, ...), condition=%wide.region_52.53_spmd, body=%wide.region_45.52_spmd.sunk | while | flops 85970952 | bytes 499925 | solution.py:37
  1078.0 16.2 fusion.193
  1094.4 16.2 fusion.193
  1110.7 2.3 copy.279
  1113.6 34.0 %while.85 = (s32[]{:T(128)}, f32[2,6,2048]{2,1,0:T(8,128)}, f32[3,1024]{1,0:T(4,128)S(1)}, f32[2,6,2048]{2,1,0:T(8,128)S(1)}, f32[3,1024]{1,0:T(4,128)S(1)}, /*i...) while((s32[]{:T(128)}, f32[2,6,2048]{2,1,0:T(8,128)}, f32[3,1024]{1,0:T(4,128)S(1)}, ...), condition=%wide.region_60.61_spmd, body=%wide.region_53.60_spmd.sunk | while | flops 85970952 | bytes 483541 | solution.py:37
  1113.7 16.2 fusion.195
  1130.7 16.2 fusion.195
  1147.9 2.2 copy.282
  1150.1 32.8 %while.86 = (s32[]{:T(128)}, f32[2,6,2048]{2,1,0:T(8,128)S(1)}, f32[3,1024]{1,0:T(4,128)S(1)}, f32[2,6,2048]{2,1,0:T(8,128)S(1)}, f32[3,1024]{1,0:T(4,128)S(1)},...) while((s32[]{:T(128)}, f32[2,6,2048]{2,1,0:T(8,128)S(1)}, ...), condition=%wide.region_69.70_spmd, body=%wide.region_62.69_spmd.sunk | while | flops 85970952 | bytes 499925 | solution.py:37
  1150.2 16.2 fusion.197
  1166.6 16.2 fusion.197
  1183.7 32.8 %while.87 = (s32[]{:T(128)}, f32[2,6,2048]{2,1,0:T(8,128)S(1)}, f32[3,1024]{1,0:T(4,128)S(1)}, f32[2,6,2048]{2,1,0:T(8,128)S(1)}, f32[3,1024]{1,0:T(4,128)S(1)},...) while((s32[]{:T(128)}, f32[2,6,2048]{2,1,0:T(8,128)S(1)}, ...), condition=%wide.region_78.79_spmd, body=%wide.region_71.78_spmd.sunk | while | flops 85970952 | bytes 499925 | solution.py:37
  1183.8 16.2 fusion.199
  1200.2 16.2 fusion.199
  1219.8 66.7 %all-reduce.17.cloned.1.call-done = f32[6,4096]{1,0:T(8,128)} async-done(((f32[6,4096]{1,0:T(8,128)}), f32[6,4096]{1,0:T(8,128)}) %all-reduce.17.cloned.1.call-update) | async-done | bytes 98320 | tf_op jit(solution)/shard_map/psum | solution.py:96
  1287.5 141.8 %all-reduce.19.cloned.1.call-done = f32[6,4096]{1,0:T(8,128)} async-done(((f32[6,4096]{1,0:T(8,128)}), f32[6,4096]{1,0:T(8,128)}) %all-reduce.19.cloned.1.call-update) | async-done | bytes 98320 | tf_op jit(solution)/shard_map/psum | solution.py:96
  1430.3 141.2 %all-reduce.21.cloned.1.call-done = f32[6,4096]{1,0:T(8,128)} async-done(((f32[6,4096]{1,0:T(8,128)}), f32[6,4096]{1,0:T(8,128)}) %all-reduce.21.cloned.1.call-update) | async-done | bytes 98320 | tf_op jit(solution)/shard_map/psum | solution.py:96
  1571.5 0.9 constant_dynamic-update-slice_fusion.7
  1572.5 142.0 %all-reduce.23.cloned.1.call-done = f32[6,4096]{1,0:T(8,128)} async-done(((f32[6,4096]{1,0:T(8,128)}), f32[6,4096]{1,0:T(8,128)}) %all-reduce.23.cloned.1.call-update) | async-done | bytes 98320 | tf_op jit(solution)/shard_map/psum | solution.py:96
  1715.6 1.4 scatter_fusion.5
  1717.9 1.4 scatter_fusion.6
  1720.2 1.4 scatter_fusion.7
  1722.6 1.4 scatter_fusion.8
  (218 shorter events, 34.7 us)
Async XLA Ops:
  7.2 501.2 %all-reduce.9.cloned.1.call-start = ((), (), s32[]{:S(2)}) async-start(), calls=%async_computation | async-start | bytes 262144 | tf_op jit(solution)/shard_map/psum | solution.py:96
  78.7 11.5 copy-start.18
  289.1 0.6 copy-start.5
  289.8 357.4 %all-reduce.11.cloned.1.call-start = ((), (), s32[]{:S(2)}) async-start(), calls=%async_computation.1 | async-start | bytes 262144 | tf_op jit(solution)/shard_map/psum | solution.py:96
  327.5 2.3 copy-start.6
  362.7 0.7 copy-start.7
  396.2 100.8 %copy-start.8 = (f32[2,6,2048]{2,1,0:T(8,128)}, f32[2,6,2048]{2,1,0:T(8,128)S(1)}, u32[]{:S(2)}) copy-start(f32[2,6,2048]{2,1,0:T(8,128)S(1)} %get-tuple-element.238) | copy-start | bytes 294916
  397.6 543.1 %copy-start.15 = (s32[1024]{0:T(1024)}, s32[1024]{0:T(1024)S(1)}, u32[]{:S(2)}) copy-start(s32[1024]{0:T(1024)S(1)} %pad_clamp_fusion) | copy-start | bytes 12292
  399.7 99.4 %copy-start.11 = (f32[3,1024]{1,0:T(4,128)S(1)}, f32[3,1024]{1,0:T(4,128)}, u32[]{:S(2)}) copy-start(f32[3,1024]{1,0:T(4,128)} %param.23) | copy-start | bytes 36868
  399.7 99.6 %copy-start.12 = (f32[3,1024]{1,0:T(4,128)S(1)}, f32[3,1024]{1,0:T(4,128)}, u32[]{:S(2)}) copy-start(f32[3,1024]{1,0:T(4,128)} %param.25) | copy-start | bytes 36868
  399.7 99.8 %copy-start.13 = (f32[3,1024]{1,0:T(4,128)S(1)}, f32[3,1024]{1,0:T(4,128)}, u32[]{:S(2)}) copy-start(f32[3,1024]{1,0:T(4,128)} %param.24) | copy-start | bytes 36868
  399.7 100.7 %copy-start.14 = (f32[3,1024]{1,0:T(4,128)S(1)}, f32[3,1024]{1,0:T(4,128)}, u32[]{:S(2)}) copy-start(f32[3,1024]{1,0:T(4,128)} %param.26) | copy-start | bytes 36868
  508.4 281.0 %all-reduce.13.cloned.1.call-start = ((), (), s32[]{:S(2)}) async-start(), calls=%async_computation.2 | async-start | bytes 262144 | tf_op jit(solution)/shard_map/psum | solution.py:96
  647.2 285.0 %all-reduce.15.cloned.1.call-start = ((), (), s32[]{:S(2)}) async-start(), calls=%async_computation.3 | async-start | bytes 262144 | tf_op jit(solution)/shard_map/psum | solution.py:96
  789.4 497.1 %all-reduce.17.cloned.1.call-start = ((), (), s32[]{:S(2)}) async-start(), calls=%async_computation.4 | async-start | bytes 262144 | tf_op jit(solution)/shard_map/psum | solution.py:96
  934.7 74.5 %copy-start.2 = (f32[3,1024]{0,1:T(8,128)}, f32[3,1024]{0,1:T(8,128)S(1)}, u32[]{:S(2)}) copy-start(f32[3,1024]{0,1:T(8,128)S(1)} %scatter_fusion) | copy-start | bytes 36868
  936.3 73.0 %copy-start = (f32[3,1024]{0,1:T(8,128)}, f32[3,1024]{0,1:T(8,128)S(1)}, u32[]{:S(2)}) copy-start(f32[3,1024]{0,1:T(8,128)S(1)} %scatter_fusion.3) | copy-start | bytes 36868
  1110.7 2.9 copy-start.9
  1147.6 281.7 %all-reduce.19.cloned.1.call-start = ((), (), s32[]{:S(2)}) async-start(), calls=%async_computation.5 | async-start | bytes 262144 | tf_op jit(solution)/shard_map/psum | solution.py:96
  1183.0 0.7 copy-start.10
  1183.6 32.9 %copy-start.1 = (f32[3,1024]{0,1:T(8,128)S(1)}, f32[3,1024]{0,1:T(8,128)}, u32[]{:S(2)}) copy-start(f32[3,1024]{0,1:T(8,128)} %copy-done) | copy-start | bytes 36868
  1183.6 32.9 %copy-start.16 = (s32[1024]{0:T(1024)S(1)}, s32[1024]{0:T(1024)}, u32[]{:S(2)}) copy-start(s32[1024]{0:T(1024)} %copy-done.15) | copy-start | bytes 12292
  1183.6 34.3 %copy-start.3 = (f32[3,1024]{0,1:T(8,128)S(1)}, f32[3,1024]{0,1:T(8,128)}, u32[]{:S(2)}) copy-start(f32[3,1024]{0,1:T(8,128)} %copy-done.2) | copy-start | bytes 36868
  1183.6 531.7 %copy-start.19 = (f32[256]{0:T(256)S(1)}, f32[256]{0:T(256)}, u32[]{:S(2)}) copy-start(f32[256]{0:T(256)} %get-tuple-element.731) | copy-start | bytes 3076
  1183.6 531.7 %copy-start.20 = (f32[256]{0:T(256)S(1)}, f32[256]{0:T(256)}, u32[]{:S(2)}) copy-start(f32[256]{0:T(256)} %get-tuple-element.732) | copy-start | bytes 3076
  1183.7 531.9 %copy-start.17 = (s32[256,1]{0,1:T(1,128)S(1)}, s32[256,1]{0,1:T(1,128)}, u32[]{:S(2)}) copy-start(s32[256,1]{0,1:T(1,128)} %get-tuple-element.729) | copy-start | bytes 3076
  1216.5 355.0 %copy-start.4 = (f32[2,6,2048]{2,1,0:T(8,128)}, f32[2,6,2048]{2,1,0:T(8,128)S(1)}, u32[]{:S(2)}) copy-start(f32[2,6,2048]{2,1,0:T(8,128)S(1)} %get-tuple-element.248) | copy-start | bytes 294916
  1286.5 285.0 %all-reduce.21.cloned.1.call-start = ((), (), s32[]{:S(2)}) async-start(), calls=%async_computation.6 | async-start | bytes 262144 | tf_op jit(solution)/shard_map/psum | solution.py:96
  1429.3 285.1 %all-reduce.23.cloned.1.call-start = ((), (), s32[]{:S(2)}) async-start(), calls=%async_computation.7 | async-start | bytes 262144 | tf_op jit(solution)/shard_map/psum | solution.py:96
Sparse Core Ops, SparseCore 0:
  289.9 138.5 all-reduce.8
  508.5 138.5 all-reduce.10
  651.9 137.4 all-reduce.12
  794.7 137.4 all-reduce.14
  1147.8 138.6 all-reduce.16
  1291.8 137.4 all-reduce.18
  1434.0 137.4 all-reduce.20
  1577.0 137.4 all-reduce.22
where the time goes:
time: 1740 us; the launch traced here: 1730 us
  waiting for transfers between devices  913 us (52%)
  local copies, waits for them, and re-layouts  405 us (23%)
  other arithmetic  270 us (16%)
  blocking collectives  123 us (7%)
  between operations  19 us (1%)
    psum x8, waiting for transfers between devices, shards(): summed = lax.psum(terms, ('grp', 'dev'))  913 us
    reduce_sum x16, other arithmetic, pair_block(): jnp.sum(weight * (drift_z - along * gap_z), axis=1)  259 us
    gather x2, local copies, waits for them, and re-layouts, shards(): slot = owner * slot_cap + place - first[owner]  194 us
    all_gather x2, blocking collectives, shards(): gathered = lax.all_gather(targets[None], ('grp', 'dev'), axis=0, tiled=True)  123 us
    gather x2, local copies, waits for them, and re-layouts, shards(): compact = flat[:, slot]  120 us
  transfers between devices with their start and end apart: 8, of which 7 were waited for; matrix products, arithmetic and copies ran while one was open for 17% of the time, Pallas kernels for 0%

commit v1 on v0

--- a/solution.py
+++ b/solution.py
@@ -82,7 +82,11 @@
         owner = jnp.sum((inclusive[None, :] <= place[:, None]).astype(jnp.int32), axis=1)
         owner = jnp.minimum(owner, devices_all - 1)
         slot = owner * slot_cap + place - first[owner]
-        gathered = lax.all_gather(targets[None], ("grp", "dev"), axis=0, tiled=True)
+        part = targets[None]
+        size = lax.axis_size(("grp", "dev"))
+        blocks = jnp.stack([part for _ in range(size)])
+        blocks = lax.all_to_all(blocks, ("grp", "dev"), split_axis=0, concat_axis=0)
+        gathered = jnp.concatenate(blocks, axis=0)
         flat = gathered.transpose(1, 0, 2).reshape(6, devices_all * slot_cap)
         compact = flat[:, slot]
         parts = []

time: 1740 us -> 1750 us (level)
  blocking collectives: 123 us -> 0 us
  waiting for transfers between devices: 913 us -> 988 us
  local copies, waits for them, and re-layouts: 405 us -> 431 us
  starting transfers between devices: 0.82 us -> 18.4 us
    all_gather x2 -> x0, blocking collectives: 123 us -> none  [shards(): gathered = lax.all_gather(targets[None], ('grp', 'dev'), axis=0, tiled=True)]
    psum x8, waiting for transfers between devices: 913 us -> 985 us  [shards(): summed = lax.psum(terms, ('grp', 'dev'))]
  transfers between devices with their start and end apart: 8 -> 10, of which waited for: 7 -> 9; matrix products, arithmetic and copies ran while one was open for 17% -> 22% of each run, Pallas kernels for 0% -> 0%
where the time goes in v1:
time: 1750 us; the launch traced here: 1740 us
  waiting for transfers between devices  988 us (56%)
  local copies, waits for them, and re-layouts  431 us (25%)
  other arithmetic  280 us (16%)
  between operations  19.2 us (1%)
  starting transfers between devices  18.4 us (1%)
    psum x8, waiting for transfers between devices, shards(): summed = lax.psum(terms, ('grp', 'dev'))  985 us
    reduce_sum x16, other arithmetic, pair_block(): jnp.sum(weight * (drift_z - along * gap_z), axis=1)  266 us
    gather x2, local copies, waits for them, and re-layouts, shards(): slot = owner * slot_cap + place - first[owner]  194 us
    gather x2, local copies, waits for them, and re-layouts, shards(): compact = flat[:, slot]  120 us
  transfers between devices with their start and end apart: 10, of which 9 were waited for; matrix products, arithmetic and copies ran while one was open for 22% of the time, Pallas kernels for 0%

profile of v1, /device:TPU:1, one launch (start us, length us, event | category | flops | bytes accessed | tf_op | source)
XLA Modules:
  0.0 1737.8 jit_solution(6084078195157226343)
XLA Ops:
  8.5 2.6 compare_select_fusion.4
  16.0 11.5 all-to-all-start
  32.2 2.3 convert_reduce_fusion.1
  35.3 2.3 convert_reduce_fusion
  42.5 97.2 %gather_fusion.6 = s32[16384]{0:T(1024)S(1)} fusion(s32[128]{0:T(128)S(1)} %get-tuple-element.778, s32[16384]{0:T(1024)S(1)} %broadcast_clamp_fusion.3), kind=kCustom, calls=%fused_computation.6 | custom fusion | bytes 196608 | tf_op jit(solution)/shard_map/gather | solution.py:84
  141.2 1.4 gather_fusion.1
  145.3 1.7 scatter_fusion.1
  147.0 97.2 %gather_fusion.15 = s32[16384]{0:T(1024)S(1)} fusion(s32[128]{0:T(128)S(1)} %get-tuple-element.777, s32[16384]{0:T(1024)S(1)} %broadcast_clamp_fusion.2), kind=kCustom, calls=%fused_computation.15 | custom fusion | bytes 196608 | tf_op jit(solution)/shard_map/gather | solution.py:84
  245.5 8.7 copy.361
  254.1 60.2 %gather_fusion.7 = f32[16384,6]{1,0:T(8,128)} fusion(f32[6,32768]{0,1:T(8,128)} %bitcast.634, s32[16384]{0:T(1024)S(1)} %broadcast_clamp_fusion.1), kind=kCustom, calls=%fused_computation.7 | custom fusion | bytes 851968 | tf_op jit(solution)/shard_map/gather | solution.py:91
  314.3 6.2 fusion.167
  320.5 2.2 copy.318
  323.4 36.6 %while.80 = (s32[]{:T(128)}, f32[2,6,2048]{2,1,0:T(8,128)}, f32[3,1024]{1,0:T(4,128)S(1)}, f32[2,6,2048]{2,1,0:T(8,128)S(1)}, f32[3,1024]{1,0:T(4,128)S(1)}, /*i...) while((s32[]{:T(128)}, f32[2,6,2048]{2,1,0:T(8,128)}, f32[3,1024]{1,0:T(4,128)S(1)}, ...), condition=%wide.region_9.10_spmd, body=%wide.region_2.9_spmd.sunk | while | flops 85970952 | bytes 483541 | solution.py:37
  323.5 16.8 fusion.185
  341.8 16.8 fusion.185
  360.0 2.2 copy.319
  362.9 36.6 %while.81 = (s32[]{:T(128)}, f32[2,6,2048]{2,1,0:T(8,128)}, f32[3,1024]{1,0:T(4,128)S(1)}, f32[2,6,2048]{2,1,0:T(8,128)S(1)}, f32[3,1024]{1,0:T(4,128)S(1)}, /*i...) while((s32[]{:T(128)}, f32[2,6,2048]{2,1,0:T(8,128)}, f32[3,1024]{1,0:T(4,128)S(1)}, ...), condition=%wide.region_17.18_spmd, body=%wide.region_10.17_spmd.sunk | while | flops 85970952 | bytes 483541 | solution.py:37
  363.0 16.8 fusion.187
  381.3 16.8 fusion.187
  400.1 2.2 copy.320
  403.0 36.6 %while.82 = (s32[]{:T(128)}, f32[2,6,2048]{2,1,0:T(8,128)}, f32[3,1024]{1,0:T(4,128)S(1)}, f32[2,6,2048]{2,1,0:T(8,128)S(1)}, f32[3,1024]{1,0:T(4,128)S(1)}, /*i...) while((s32[]{:T(128)}, f32[2,6,2048]{2,1,0:T(8,128)}, f32[3,1024]{1,0:T(4,128)S(1)}, ...), condition=%wide.region_26.27_spmd, body=%wide.region_19.26_spmd.sunk | while | flops 85970952 | bytes 483541 | solution.py:37
  403.1 16.8 fusion.189
  421.4 16.8 fusion.189
  440.4 32.8 %while.83 = (s32[]{:T(128)}, f32[2,6,2048]{2,1,0:T(8,128)S(1)}, f32[3,1024]{1,0:T(4,128)S(1)}, f32[2,6,2048]{2,1,0:T(8,128)S(1)}, f32[3,1024]{1,0:T(4,128)S(1)},...) while((s32[]{:T(128)}, f32[2,6,2048]{2,1,0:T(8,128)S(1)}, ...), condition=%wide.region_35.36_spmd, body=%wide.region_28.35_spmd.sunk | while | flops 85970952 | bytes 499925 | solution.py:37
  440.5 16.2 fusion.191
  456.9 16.2 fusion.191
  473.2 68.0 %all-reduce.9.cloned.1.call-done = f32[6,4096]{1,0:T(8,128)} async-done(((f32[6,4096]{1,0:T(8,128)}), f32[6,4096]{1,0:T(8,128)}) %all-reduce.9.cloned.1.call-update) | async-done | bytes 98320 | tf_op jit(solution)/shard_map/psum | solution.py:100
  542.2 142.0 %all-reduce.11.cloned.1.call-done = f32[6,4096]{1,0:T(8,128)} async-done(((f32[6,4096]{1,0:T(8,128)}), f32[6,4096]{1,0:T(8,128)}) %all-reduce.11.cloned.1.call-update) | async-done | bytes 98320 | tf_op jit(solution)/shard_map/psum | solution.py:100
  685.2 141.3 %all-reduce.13.cloned.1.call-done = f32[6,4096]{1,0:T(8,128)} async-done(((f32[6,4096]{1,0:T(8,128)}), f32[6,4096]{1,0:T(8,128)}) %all-reduce.13.cloned.1.call-update) | async-done | bytes 98320 | tf_op jit(solution)/shard_map/psum | solution.py:100
  827.4 141.9 %all-reduce.15.cloned.1.call-done = f32[6,4096]{1,0:T(8,128)} async-done(((f32[6,4096]{1,0:T(8,128)}), f32[6,4096]{1,0:T(8,128)}) %all-reduce.15.cloned.1.call-update) | async-done | bytes 98320 | tf_op jit(solution)/shard_map/psum | solution.py:100
  970.5 1.4 scatter_fusion
  972.0 1.4 scatter_fusion.3
  973.6 1.4 scatter_fusion.2
  975.1 1.4 scatter_fusion.4
  978.7 1.3 stack.175
  980.0 5.7 all-to-all-start.1
  987.9 1.4 gather_fusion.10
  998.6 3.6 all-to-all-done.1
  1002.2 8.7 copy.362
  1010.9 60.2 %gather_fusion.16 = f32[16384,6]{1,0:T(8,128)} fusion(f32[6,32768]{0,1:T(8,128)} %bitcast.635, s32[16384]{0:T(1024)S(1)} %broadcast_clamp_fusion), kind=kCustom, calls=%fused_computation.16 | custom fusion | bytes 851968 | tf_op jit(solution)/shard_map/gather | solution.py:91
  1071.1 6.2 fusion.166
  1077.2 2.2 copy.340
  1079.5 35.4 %while.84 = (s32[]{:T(128)}, f32[2,6,2048]{2,1,0:T(8,128)S(1)}, f32[3,1024]{1,0:T(4,128)S(1)}, f32[2,6,2048]{2,1,0:T(8,128)S(1)}, f32[3,1024]{1,0:T(4,128)S(1)},...) while((s32[]{:T(128)}, f32[2,6,2048]{2,1,0:T(8,128)S(1)}, ...), condition=%wide.region_52.53_spmd, body=%wide.region_45.52_spmd.sunk | while | flops 85970952 | bytes 499925 | solution.py:37
  1079.6 16.8 fusion.193
  1097.3 16.8 fusion.193
  1114.9 2.3 copy.343
  1117.8 36.5 %while.85 = (s32[]{:T(128)}, f32[2,6,2048]{2,1,0:T(8,128)}, f32[3,1024]{1,0:T(4,128)S(1)}, f32[2,6,2048]{2,1,0:T(8,128)S(1)}, f32[3,1024]{1,0:T(4,128)S(1)}, /*i...) while((s32[]{:T(128)}, f32[2,6,2048]{2,1,0:T(8,128)}, f32[3,1024]{1,0:T(4,128)S(1)}, ...), condition=%wide.region_60.61_spmd, body=%wide.region_53.60_spmd.sunk | while | flops 85970952 | bytes 483541 | solution.py:37
  1117.9 16.8 fusion.195
  1136.2 16.8 fusion.195
  1154.6 2.2 copy.346
  1156.9 35.4 %while.86 = (s32[]{:T(128)}, f32[2,6,2048]{2,1,0:T(8,128)S(1)}, f32[3,1024]{1,0:T(4,128)S(1)}, f32[2,6,2048]{2,1,0:T(8,128)S(1)}, f32[3,1024]{1,0:T(4,128)S(1)},...) while((s32[]{:T(128)}, f32[2,6,2048]{2,1,0:T(8,128)S(1)}, ...), condition=%wide.region_69.70_spmd, body=%wide.region_62.69_spmd.sunk | while | flops 85970952 | bytes 499925 | solution.py:37
  1157.0 16.8 fusion.197
  1174.7 16.8 fusion.197
  1193.0 32.9 %while.87 = (s32[]{:T(128)}, f32[2,6,2048]{2,1,0:T(8,128)S(1)}, f32[3,1024]{1,0:T(4,128)S(1)}, f32[2,6,2048]{2,1,0:T(8,128)S(1)}, f32[3,1024]{1,0:T(4,128)S(1)},...) while((s32[]{:T(128)}, f32[2,6,2048]{2,1,0:T(8,128)S(1)}, ...), condition=%wide.region_78.79_spmd, body=%wide.region_71.78_spmd.sunk | while | flops 85970952 | bytes 499925 | solution.py:37
  1193.1 16.2 fusion.199
  1209.5 16.2 fusion.199
  1225.9 66.6 %all-reduce.17.cloned.1.call-done = f32[6,4096]{1,0:T(8,128)} async-done(((f32[6,4096]{1,0:T(8,128)}), f32[6,4096]{1,0:T(8,128)}) %all-reduce.17.cloned.1.call-update) | async-done | bytes 98320 | tf_op jit(solution)/shard_map/psum | solution.py:100
  1293.4 141.8 %all-reduce.19.cloned.1.call-done = f32[6,4096]{1,0:T(8,128)} async-done(((f32[6,4096]{1,0:T(8,128)}), f32[6,4096]{1,0:T(8,128)}) %all-reduce.19.cloned.1.call-update) | async-done | bytes 98320 | tf_op jit(solution)/shard_map/psum | solution.py:100
  1436.2 141.2 %all-reduce.21.cloned.1.call-done = f32[6,4096]{1,0:T(8,128)} async-done(((f32[6,4096]{1,0:T(8,128)}), f32[6,4096]{1,0:T(8,128)}) %all-reduce.21.cloned.1.call-update) | async-done | bytes 98320 | tf_op jit(solution)/shard_map/psum | solution.py:100
  1578.4 142.0 %all-reduce.23.cloned.1.call-done = f32[6,4096]{1,0:T(8,128)} async-done(((f32[6,4096]{1,0:T(8,128)}), f32[6,4096]{1,0:T(8,128)}) %all-reduce.23.cloned.1.call-update) | async-done | bytes 98320 | tf_op jit(solution)/shard_map/psum | solution.py:100
  1721.6 1.4 scatter_fusion.5
  1723.9 1.4 scatter_fusion.6
  1726.3 1.4 scatter_fusion.7
  1728.6 1.4 scatter_fusion.8
  (246 shorter events, 64.6 us)
Async XLA Ops:
  11.1 134.2 %copy-start.14 = (s32[256,1]{0,1:T(1,128)}, s32[256,1]{0,1:T(1,128)S(1)}, u32[]{:S(2)}) copy-start(s32[256,1]{0,1:T(1,128)S(1)} %get-tuple-element.774) | copy-start | bytes 3076
  16.0 229.4 %all-to-all-start = ((f32[128,1,6,256]{3,1,2,0:T(1,128)}), f32[128,1,6,256]{3,1,2,0:T(1,128)S(1)}, u32[]{:S(2)}, u32[]{:S(2)}) async-start(f32[128,1,6,256]{3,1,2,0:T(1,128)} %stack.174), calls=%async_computation | async-start | bytes 1572864 | tf_op jit(solution)/shard_map/all_to_all | solution.py:88
  27.5 513.7 %all-reduce.9.cloned.1.call-start = ((), (), s32[]{:S(2)}) async-start(), calls=%async_computation.2 | async-start | bytes 262144 | tf_op jit(solution)/shard_map/psum | solution.py:100
  28.5 111.2 %copy-start.4 = (f32[3,1024]{0,1:T(8,128)}, f32[3,1024]{0,1:T(8,128)S(1)}, u32[]{:S(2)}) copy-start(f32[3,1024]{0,1:T(8,128)S(1)} %copy.324) | copy-start | bytes 36868
  29.5 110.3 %copy-start = (f32[3,1024]{0,1:T(8,128)}, f32[3,1024]{0,1:T(8,128)S(1)}, u32[]{:S(2)}) copy-start(f32[3,1024]{0,1:T(8,128)S(1)} %copy.309) | copy-start | bytes 36868
  399.5 284.7 %all-reduce.11.cloned.1.call-start = ((), (), s32[]{:S(2)}) async-start(), calls=%async_computation.3 | async-start | bytes 262144 | tf_op jit(solution)/shard_map/psum | solution.py:100
  440.2 529.9 %copy-start.21 = (f32[256,3]{0,1:T(4,128)S(1)}, f32[256,3]{0,1:T(4,128)}, u32[]{:S(2)}) copy-start(f32[256,3]{0,1:T(4,128)} %copy.310) | copy-start | bytes 9220
  440.3 529.9 %copy-start.22 = (f32[256,3]{0,1:T(4,128)S(1)}, f32[256,3]{0,1:T(4,128)}, u32[]{:S(2)}) copy-start(f32[256,3]{0,1:T(4,128)} %copy.308) | copy-start | bytes 9220
  440.3 529.9 %copy-start.23 = (f32[256,3]{0,1:T(4,128)S(1)}, f32[256,3]{0,1:T(4,128)}, u32[]{:S(2)}) copy-start(f32[256,3]{0,1:T(4,128)} %copy.306) | copy-start | bytes 9220
  440.3 529.9 %copy-start.24 = (f32[256,3]{0,1:T(4,128)S(1)}, f32[256,3]{0,1:T(4,128)}, u32[]{:S(2)}) copy-start(f32[256,3]{0,1:T(4,128)} %copy.323) | copy-start | bytes 9220
  440.3 529.9 %copy-start.29 = (f32[256]{0:T(256)S(1)}, f32[256]{0:T(256)}, u32[]{:S(2)}) copy-start(f32[256]{0:T(256)} %get-tuple-element.783) | copy-start | bytes 3076
  440.3 529.9 %copy-start.30 = (f32[256]{0:T(256)S(1)}, f32[256]{0:T(256)}, u32[]{:S(2)}) copy-start(f32[256]{0:T(256)} %get-tuple-element.784) | copy-start | bytes 3076
  440.3 530.2 %copy-start.5 = (f32[3,1024]{0,1:T(8,128)S(1)}, f32[3,1024]{0,1:T(8,128)}, u32[]{:S(2)}) copy-start(f32[3,1024]{0,1:T(8,128)} %copy-done.4) | copy-start | bytes 36868
  440.3 530.2 %copy-start.15 = (s32[256,1]{0,1:T(1,128)S(1)}, s32[256,1]{0,1:T(1,128)}, u32[]{:S(2)}) copy-start(s32[256,1]{0,1:T(1,128)} %copy-done.14) | copy-start | bytes 3076
  440.3 531.7 %copy-start.1 = (f32[3,1024]{0,1:T(8,128)S(1)}, f32[3,1024]{0,1:T(8,128)}, u32[]{:S(2)}) copy-start(f32[3,1024]{0,1:T(8,128)} %copy-done) | copy-start | bytes 36868
  440.3 536.1 %copy-start.18 = (f32[1024]{0:T(1024)S(1)}, f32[1024]{0:T(1024)}, u32[]{:S(2)}) copy-start(f32[1024]{0:T(1024)} %get-tuple-element.764) | copy-start | bytes 12292
  440.4 536.1 %copy-start.19 = (f32[1024]{0:T(1024)S(1)}, f32[1024]{0:T(1024)}, u32[]{:S(2)}) copy-start(f32[1024]{0:T(1024)} %get-tuple-element.765) | copy-start | bytes 12292
  440.4 536.1 %copy-start.20 = (f32[1024]{0:T(1024)S(1)}, f32[1024]{0:T(1024)}, u32[]{:S(2)}) copy-start(f32[1024]{0:T(1024)} %get-tuple-element.766) | copy-start | bytes 12292
  440.4 536.6 %copy-start.16 = (s32[1024]{0:T(1024)S(1)}, s32[1024]{0:T(1024)}, u32[]{:S(2)}) copy-start(s32[1024]{0:T(1024)} %pad_clamp_fusion) | copy-start | bytes 12292
  473.2 353.2 %copy-start.11 = (f32[2,6,2048]{2,1,0:T(8,128)}, f32[2,6,2048]{2,1,0:T(8,128)S(1)}, u32[]{:S(2)}) copy-start(f32[2,6,2048]{2,1,0:T(8,128)S(1)} %get-tuple-element.238) | copy-start | bytes 294916
  541.3 285.2 %all-reduce.13.cloned.1.call-start = ((), (), s32[]{:S(2)}) async-start(), calls=%async_computation.4 | async-start | bytes 262144 | tf_op jit(solution)/shard_map/psum | solution.py:100
  684.2 285.0 %all-reduce.15.cloned.1.call-start = ((), (), s32[]{:S(2)}) async-start(), calls=%async_computation.5 | async-start | bytes 262144 | tf_op jit(solution)/shard_map/psum | solution.py:100
  971.9 39.0 %copy-start.6 = (f32[3,1024]{0,1:T(8,128)}, f32[3,1024]{0,1:T(8,128)S(1)}, u32[]{:S(2)}) copy-start(f32[3,1024]{0,1:T(8,128)S(1)} %scatter_fusion) | copy-start | bytes 36868
  973.4 37.5 %copy-start.2 = (f32[3,1024]{0,1:T(8,128)}, f32[3,1024]{0,1:T(8,128)S(1)}, u32[]{:S(2)}) copy-start(f32[3,1024]{0,1:T(8,128)S(1)} %scatter_fusion.3) | copy-start | bytes 36868
  977.0 3.0 copy-start.8
  977.0 3.0 copy-start.9
  980.0 22.2 %all-to-all-start.1 = ((f32[128,1,6,256]{3,1,2,0:T(1,128)}), f32[128,1,6,256]{3,1,2,0:T(1,128)S(1)}, u32[]{:S(2)}, u32[]{:S(2)}) async-start(f32[128,1,6,256]{3,1,2,0:T(1,128)} %stack.175), calls=%async_computation.1 | async-start | bytes 1572864 | tf_op jit(solution)/shard_map/all_to_all | solution.py:88
  985.6 306.8 %all-reduce.17.cloned.1.call-start = ((), (), s32[]{:S(2)}) async-start(), calls=%async_computation.6 | async-start | bytes 262144 | tf_op jit(solution)/shard_map/psum | solution.py:100
  1114.9 2.9 copy-start.12
  1154.4 280.9 %all-reduce.19.cloned.1.call-start = ((), (), s32[]{:S(2)}) async-start(), calls=%async_computation.7 | async-start | bytes 262144 | tf_op jit(solution)/shard_map/psum | solution.py:100
  1192.2 0.8 copy-start.13
  1192.9 528.4 %copy-start.25 = (f32[256,3]{0,1:T(4,128)S(1)}, f32[256,3]{0,1:T(4,128)}, u32[]{:S(2)}) copy-start(f32[256,3]{0,1:T(4,128)} %copy.332) | copy-start | bytes 9220
  1192.9 528.4 %copy-start.26 = (f32[256,3]{0,1:T(4,128)S(1)}, f32[256,3]{0,1:T(4,128)}, u32[]{:S(2)}) copy-start(f32[256,3]{0,1:T(4,128)} %copy.329) | copy-start | bytes 9220
  1192.9 528.4 %copy-start.27 = (f32[256,3]{0,1:T(4,128)S(1)}, f32[256,3]{0,1:T(4,128)}, u32[]{:S(2)}) copy-start(f32[256,3]{0,1:T(4,128)} %copy.326) | copy-start | bytes 9220
  1192.9 528.4 %copy-start.28 = (f32[256,3]{0,1:T(4,128)S(1)}, f32[256,3]{0,1:T(4,128)}, u32[]{:S(2)}) copy-start(f32[256,3]{0,1:T(4,128)} %copy.352) | copy-start | bytes 9220
  1193.0 528.4 %copy-start.31 = (f32[256]{0:T(256)S(1)}, f32[256]{0:T(256)}, u32[]{:S(2)}) copy-start(f32[256]{0:T(256)} %get-tuple-element.775) | copy-start | bytes 3076
  1193.0 528.4 %copy-start.32 = (f32[256]{0:T(256)S(1)}, f32[256]{0:T(256)}, u32[]{:S(2)}) copy-start(f32[256]{0:T(256)} %get-tuple-element.776) | copy-start | bytes 3076
  1193.0 528.6 %copy-start.7 = (f32[3,1024]{0,1:T(8,128)S(1)}, f32[3,1024]{0,1:T(8,128)}, u32[]{:S(2)}) copy-start(f32[3,1024]{0,1:T(8,128)} %copy-done.6) | copy-start | bytes 36868
  1193.0 528.6 %copy-start.17 = (s32[256,1]{0,1:T(1,128)S(1)}, s32[256,1]{0,1:T(1,128)}, u32[]{:S(2)}) copy-start(s32[256,1]{0,1:T(1,128)} %get-tuple-element.773) | copy-start | bytes 3076
  1193.0 533.3 %copy-start.3 = (f32[3,1024]{0,1:T(8,128)S(1)}, f32[3,1024]{0,1:T(8,128)}, u32[]{:S(2)}) copy-start(f32[3,1024]{0,1:T(8,128)} %copy-done.2) | copy-start | bytes 36868
  1225.9 351.6 %copy-start.10 = (f32[2,6,2048]{2,1,0:T(8,128)}, f32[2,6,2048]{2,1,0:T(8,128)S(1)}, u32[]{:S(2)}) copy-start(f32[2,6,2048]{2,1,0:T(8,128)S(1)} %get-tuple-element.248) | copy-start | bytes 294916
  1292.5 285.0 %all-reduce.21.cloned.1.call-start = ((), (), s32[]{:S(2)}) async-start(), calls=%async_computation.8 | async-start | bytes 262144 | tf_op jit(solution)/shard_map/psum | solution.py:100
  1435.3 285.1 %all-reduce.23.cloned.1.call-start = ((), (), s32[]{:S(2)}) async-start(), calls=%async_computation.9 | async-start | bytes 262144 | tf_op jit(solution)/shard_map/psum | solution.py:100
Sparse Core Ops, SparseCore 0:
  399.6 141.5 all-reduce.8
  546.7 137.4 all-reduce.10
  688.9 137.4 all-reduce.12
  831.8 137.4 all-reduce.14
  1154.5 137.9 all-reduce.16
  1297.8 137.4 all-reduce.18
  1440.0 137.4 all-reduce.20
  1582.9 137.4 all-reduce.22
